TPU v7x, 32 devices: a whole 2x2x4 slice. The times are simulated.
32 devices in a mesh: rep: 4 (over x, core), dev: 8 (over z, y).
Axes of the slice: x: 2, y: 2, z: 4, core: 2. Of those that a mesh axis runs over, the one named last changes fastest.
Arguments:
- group_weights: bfloat16 [4, 160, 128, 1024], P('rep', None, 'dev'), may hold values from -6 to 6
- owner: int32 [160], replicated, may hold values from 0 to 7, as said below
- start_weights: float32 [8, 40, 128, 1024], P('dev', None, None, 'rep'), may hold values from -6 to 6
- momentum: float32 [8, 40, 128, 1024], P('dev', None, None, 'rep'), may hold values from -6 to 6
- basis: float32 [64, 1024], replicated, may hold values from -1 to 1
- vec_groups: bfloat16 [4, 13, 1024], P('rep'), may hold values from -6 to 6
- vec_start: float32 [13, 1024], replicated, may hold values from -6 to 6
- vec_momentum: float32 [13, 1024], replicated, may hold values from -6 to 6
Outputs:
- new_start: float32 [8, 40, 128, 1024], P('dev', None, None, 'rep')
- new_momentum: float32 [8, 40, 128, 1024], P('dev', None, None, 'rep')
- returned: bfloat16 [160, 128, 1024], P(None, 'dev')
- vec_new: float32 [13, 1024], replicated
- vec_new_momentum: float32 [13, 1024], replicated
Inputs may be any that keep to these rules, and one draw needn't show every extreme that they name: `owner`: each index along dev owns at most 40 blocks, and some index owns exactly 40.
All inputs are finite; a program needn't handle non-finite values.
Results may differ from a plain program's by a relative error of at most 0.012.
Values may be sent and summed in bfloat16 or wider, within the bound.
No kernel may reach another device: no remote copies, remote signals or barrier semaphores. Data moves between devices by JAX's collectives and lax.ppermute only.
A program may use at most 128 MiB of HBM per device.

v0:
```python
import jax
import jax.numpy as jnp
from jax import lax
from jax.sharding import PartitionSpec as P

EMB_FIRST = 96
outer_rate = 0.7
outer_momentum = 0.9


def body(group_weights, owner, start_weights, momentum, basis, vec_groups, vec_start, vec_momentum):
    dev_count = lax.axis_size("dev")
    rep_count = lax.axis_size("rep")
    unit_count = owner.shape[0]
    slot_count = start_weights.shape[1]
    quarter = start_weights.shape[3]
    unit_ids = jnp.arange(unit_count, dtype=jnp.int32)
    same_owner = owner[:, None] == owner[None, :]
    earlier = unit_ids[None, :] < unit_ids[:, None]
    slot_of = jnp.sum((same_owner & earlier).astype(jnp.int32), axis=1)
    target = owner * slot_count + slot_of
    positions = jnp.arange(dev_count * slot_count, dtype=jnp.int32)
    placed = target[:, None] == positions[None, :]
    filled = jnp.any(placed, axis=0)
    source_unit = jnp.sum(jnp.where(placed, unit_ids[:, None], 0), axis=0)
    own_rows = group_weights[0]
    picked = jnp.take(own_rows, source_unit, axis=0)
    picked = jnp.where(filled[:, None, None], picked, jnp.zeros((), own_rows.dtype))
    arrived = lax.all_to_all(
        picked.reshape(dev_count, slot_count, own_rows.shape[1], own_rows.shape[2]),
        "dev",
        split_axis=0,
        concat_axis=2,
        tiled=True,
    )
    summed = lax.psum_scatter(
        arrived[0].astype(jnp.float32).astype(jnp.bfloat16), "rep", scatter_dimension=2, tiled=True
    ).astype(jnp.float32)
    group_mean = summed / rep_count
    start_rows = start_weights[0]
    momentum_rows = momentum[0]
    my_slots = lax.axis_index("dev") * slot_count + jnp.arange(slot_count, dtype=jnp.int32)
    own_placed = target[:, None] == my_slots[None, :]
    is_owned = jnp.any(own_placed, axis=0)
    is_embedding = jnp.any(own_placed & (unit_ids >= EMB_FIRST)[:, None], axis=0)
    change = start_rows - group_mean
    first_column = lax.axis_index("rep") * quarter
    basis_part = lax.dynamic_slice_in_dim(basis, first_column, quarter, 1)
    coeff_terms = jnp.einsum("sbq,kq->sbk", change, basis_part, precision=lax.Precision.HIGHEST)
    vec_terms = vec_groups[0].astype(jnp.float32)
    coeffs, vec_summed = (
        lax.psum(coeff_terms.astype(jnp.bfloat16), "rep").astype(jnp.float32),
        lax.psum(vec_terms.astype(jnp.bfloat16), "rep").astype(jnp.float32),
    )
    projected = jnp.einsum("sbk,kq->sbq", coeffs, basis_part, precision=lax.Precision.HIGHEST)
    outer_grad = jnp.where(is_embedding[:, None, None], projected, change)
    fresh_momentum = outer_momentum * momentum_rows + outer_grad
    fresh_start = start_rows - outer_rate * (outer_grad + outer_momentum * fresh_momentum)
    owned_mask = is_owned[:, None, None]
    new_momentum = jnp.where(owned_mask, fresh_momentum, momentum_rows)
    new_start = jnp.where(owned_mask, fresh_start, start_rows)
    rounded = fresh_start.astype(jnp.bfloat16)
    pieces = lax.all_to_all(rounded, "dev", split_axis=1, concat_axis=0, tiled=True)
    picked = jnp.take(pieces, target, axis=0)
    returned = lax.all_gather(picked, "rep", axis=2, tiled=True)
    vec_change = vec_start - vec_summed / rep_count
    vec_new_momentum = outer_momentum * vec_momentum + vec_change
    vec_new = vec_start - outer_rate * (vec_change + outer_momentum * vec_new_momentum)
    return (new_start[None], new_momentum[None], returned, vec_new, vec_new_momentum)


def solution(mesh):
    return jax.shard_map(
        body,
        mesh=mesh,
        in_specs=(
            P("rep", None, "dev", None),
            P(),
            P("dev", None, None, "rep"),
            P("dev", None, None, "rep"),
            P(),
            P("rep", None, None),
            P(),
            P(),
        ),
        out_specs=(
            P("dev", None, None, "rep"),
            P("dev", None, None, "rep"),
            P(None, "dev", None),
            P(),
            P(),
        ),
        check_vma=False,
    )
```

profile of v0, /device:TPU:0, one launch (start us, length us, event | category | flops | bytes accessed | tf_op | source)
XLA Modules:
  0.0 537.6 jit_solution(10734063896174378784)
XLA Ops:
  7.2 0.0 copy-start
  7.2 0.0 reduce-scatter.2.cloned.1.call-start
  7.2 0.9 convert_reduce_fusion
  8.2 0.7 compare_and_fusion.2
  8.9 0.1 select_reduce_fusion
  9.0 0.1 reduce_sum.24
  9.1 0.1 fusion.7
  9.2 0.1 broadcast_in_dim.85
  9.3 13.1 %gather_fusion = bf16[320,16,1024]{2,1,0:T(8,128)(2,1)} fusion(bf16[160,16,1024]{2,1,0:T(8,128)(2,1)} %bitcast.60, s32[1024]{0:T(1024)S(1)} %pad_clamp_fusion.1), kind=kCustom, calls=%fused_computation | custom fusion | bytes 20972800 | tf_op jit(solution)/shard_map/jit(_take)/gather | solution.py:27
  22.4 6.0 %select_select_fusion = bf16[8,40,16,1024]{3,2,1,0:T(8,128)(2,1)S(1)} fusion(bf16[8,40,16,1024]{3,2,1,0:T(8,128)(2,1)} %bitcast.59, pred[8,40]{1,0:T(8,128)(4,1)S(1)} %compare_and_fusion.1, pred[8,40]{1,0:T(8,128)(4,1)S(1)} %broadcast_in_dim.85), kind=kLoop, calls=%fused_computation.2 | loop fusion | flops 10485760 | bytes 20972160 | tf_op jit(solution)/shard_map/jit(_where)/select_n | solution.py:28
  28.3 235.2 %all_to_all.33 = bf16[8,40,16,1024]{3,2,1,0:T(8,128)(2,1)} all-to-all(bf16[8,40,16,1024]{3,2,1,0:T(8,128)(2,1)S(1)} %select_select_fusion), channel_id=1, replica_groups=mesh['rep'=4,'dev'=8] {'dev'}, dimensions={0} | all-to-all | bytes 20971520 | tf_op jit(solution)/shard_map/all_to_all | solution.py:29
  263.5 10.4 %copy.24 = bf16[1,40,8,16,1024]{4,3,2,1,0:T(8,128)(2,1)} copy(bf16[1,40,8,16,1024]{4,3,1,2,0:T(8,128)(2,1)} %bitcast.58) | data formatting | bytes 20971520 | tf_op jit(solution)/shard_map/all_to_all | solution.py:29
  274.0 0.0 reduce-scatter.2.cloned.1.call-update
  274.0 0.0 all-reduce.2.cloned.1.call-start
  274.0 84.4 %reduce-scatter.2.cloned.1.call-done = bf16[40,128,256]{2,1,0:T(8,128)(2,1)} async-done(((bf16[40,128,1024]{2,1,0:T(8,128)(2,1)}), bf16[40,128,256]{2,1,0:T(8,128)(2,1)}) %reduce-scatter.2.cloned.1.call-update) | async-done | bytes 2621456 | tf_op jit(solution)/shard_map/reduce_scatter | solution.py:36
  358.5 9.5 %fusion.6 = bf16[40,128,64]{1,2,0:T(8,128)(2,1)} fusion(f32[1,40,128,256]{3,2,1,0:T(8,128)} %param.10, bf16[40,128,256]{2,1,0:T(8,128)(2,1)} %reduce-scatter.2.cloned.1.call-done, f32[64,1024]{1,0:T(8,128)S(1)} %copy-done, s32[]{:T(128)S(6)} %select_n.58), kind=kOutput, calls=%fused_computation.14 | convolution fusion | flops 1010892800 | bytes 8585220 | tf_op jit(solution)/shard_map/sbq,kq->sbk/dot_general | solution.py:49
  368.0 0.0 all-reduce.2.cloned.1.call-update
  368.0 0.2 fusion.14
  368.2 33.7 %all-reduce.2.cloned.1.call-done = bf16[40,128,64]{1,2,0:T(8,128)(2,1)} async-done(((bf16[40,128,64]{1,2,0:T(8,128)(2,1)}), bf16[40,128,64]{1,2,0:T(8,128)(2,1)}) %all-reduce.2.cloned.1.call-update) | async-done | bytes 655376 | tf_op jit(solution)/shard_map/psum | solution.py:52
  401.9 10.2 %fusion.1 = (f32[1,40,128,256]{3,2,1,0:T(8,128)}, f32[1,40,128,256]{3,2,1,0:T(8,128)}, bf16[40,128,256]{2,1,0:T(8,128)(2,1)S(1)}) fusion(f32[1,40,128,256]{3,2,1,0:T(8,128)} %param.11, bf16[40,128,256]{2,1,0:T(8,128)(2,1)S(1)} %copy-done.1, f32[1,40,128,256]{3,2,1,0:T(8,128)} %param.10, pred[40]{0:T(512)(128)(4,1)S(1)} %get-tuple-element.5, ...), kind=kOutput, calls=%fused_computation.6 | convolution fusion | flops 1023672320 | bytes 26936324 | tf_op jit(solution)/shard_map/sbk,kq->sbq/dot_general | solution.py:55
  412.1 3.0 copy.25
  415.1 5.5 %all-to-all-start.1 = ((bf16[40,128,256]{2,0,1:T(8,128)(2,1)}), bf16[40,128,256]{2,0,1:T(8,128)(2,1)S(1)}, u32[]{:S(2)}, u32[]{:S(2)}) async-start(bf16[40,128,256]{2,0,1:T(8,128)(2,1)} %copy.25), calls=%async_computation.2 | async-start | bytes 5242880 | tf_op jit(solution)/shard_map/all_to_all | solution.py:63
  420.6 0.0 all-gather.2.cloned.1.call-start
  420.7 58.5 %all-to-all-done.1 = bf16[40,128,256]{2,0,1:T(8,128)(2,1)S(1)} async-done(((bf16[40,128,256]{2,0,1:T(8,128)(2,1)}), bf16[40,128,256]{2,0,1:T(8,128)(2,1)S(1)}, u32[]{:S(2)}, u32[]{:S(2)}) %all-to-all-start.1) | async-done | bytes 2621472 | tf_op jit(solution)/shard_map/all_to_all | solution.py:63
  479.2 2.1 copy.27
  481.2 2.6 gather_fusion.1
  483.8 1.3 broadcast_select_fusion
  485.1 0.0 all-gather.2.cloned.1.call-update
  485.2 10.3 %psum.15 = bf16[13,1024]{1,0:T(8,128)(2,1)S(1)} all-reduce(bf16[13,1024]{1,0:T(8,128)(2,1)S(1)} %bitcast.63), channel_id=1, replica_groups=mesh['rep'=4,'dev'=8] {'rep'}, use_global_device_ids=true, to_apply=%region_7.8 | all-reduce | flops 13312 | bytes 53248 | tf_op jit(solution)/shard_map/psum | solution.py:53
  495.5 0.7 multiply_subtract_fusion
  496.1 28.9 %all-gather.2.cloned.1.call-done = bf16[160,16,1024]{2,1,0:T(8,128)(2,1)} async-done(((bf16[160,16,256]{2,1,0:T(8,128)(2,1)}), bf16[160,16,1024]{2,1,0:T(8,128)(2,1)}) %all-gather.2.cloned.1.call-update) | async-done | bytes 5242896 | tf_op jit(solution)/shard_map/all_gather | solution.py:65
  525.1 6.0 %copy.31 = bf16[160,16,1024]{2,1,0:T(8,128)(2,1)} copy(bf16[160,16,1024]{2,1,0:T(8,128)(2,1)} %all-gather.2.cloned.1.call-done) | data formatting | bytes 10485760
  (15 shorter events, 0.1 us)
Async XLA Ops:
  7.2 351.3 %copy-start = (f32[64,1024]{1,0:T(8,128)S(1)}, f32[64,1024]{1,0:T(8,128)}, u32[]{:S(2)}) copy-start(f32[64,1024]{1,0:T(8,128)} %param.12) | copy-start | bytes 786436
  7.2 351.3 %reduce-scatter.2.cloned.1.call-start = ((), (), s32[]{:S(2)}) async-start(), calls=%async_computation.3 | async-start | bytes 13107200 | tf_op jit(solution)/shard_map/reduce_scatter | solution.py:36
  274.0 128.0 %all-reduce.2.cloned.1.call-start = ((), (), s32[]{:S(2)}) async-start(), calls=%async_computation.4 | async-start | bytes 1310720 | tf_op jit(solution)/shard_map/psum | solution.py:52
  358.5 43.5 %copy-start.1 = (bf16[40,128,256]{2,1,0:T(8,128)(2,1)S(1)}, bf16[40,128,256]{2,1,0:T(8,128)(2,1)}, u32[]{:S(2)}) copy-start(bf16[40,128,256]{2,1,0:T(8,128)(2,1)} %reduce-scatter.2.cloned.1.call-done) | copy-start | bytes 7864324
  415.1 64.1 %all-to-all-start.1 = ((bf16[40,128,256]{2,0,1:T(8,128)(2,1)}), bf16[40,128,256]{2,0,1:T(8,128)(2,1)S(1)}, u32[]{:S(2)}, u32[]{:S(2)}) async-start(bf16[40,128,256]{2,0,1:T(8,128)(2,1)} %copy.25), calls=%async_computation.2 | async-start | bytes 5242880 | tf_op jit(solution)/shard_map/all_to_all | solution.py:63
  420.6 104.5 %all-gather.2.cloned.1.call-start = ((), (), s32[]{:S(2)}) async-start(), calls=%async_computation.5 | async-start | bytes 6553600 | tf_op jit(solution)/shard_map/all_gather | solution.py:65
  479.2 6.0 %copy-start.4 = (bf16[1,13,1024]{2,1,0:T(8,128)(2,1)S(1)}, bf16[1,13,1024]{2,1,0:T(8,128)(2,1)}, u32[]{:S(2)}) copy-start(bf16[1,13,1024]{2,1,0:T(8,128)(2,1)} %param.13) | copy-start | bytes 79876
  479.2 16.3 %copy-start.2 = (f32[13,1024]{1,0:T(8,128)S(1)}, f32[13,1024]{1,0:T(8,128)}, u32[]{:S(2)}) copy-start(f32[13,1024]{1,0:T(8,128)} %param.14) | copy-start | bytes 159748
  479.2 16.3 %copy-start.3 = (f32[13,1024]{1,0:T(8,128)S(1)}, f32[13,1024]{1,0:T(8,128)}, u32[]{:S(2)}) copy-start(f32[13,1024]{1,0:T(8,128)} %param.15) | copy-start | bytes 159748
Sparse Core Ops, SparseCore 0:
  274.1 84.3 reduce-scatter.1
  368.1 33.7 all-reduce.1
  485.3 39.7 all-gather.1
where the time goes:
time: 538 us
  blocking collectives  245 us (46%)
  waiting for transfers between devices  206 us (38%)
  local copies, waits for them, and re-layouts  37.2 us (7%)
  matrix products  19.7 us (4%)
  between operations  13.9 us (3%)
  other arithmetic  10 us (2%)
  starting transfers between devices  5.63 us (1%)
    all_to_all x1, blocking collectives, body(): lax.all_to_all(picked.reshape(dev_count, slot_count, own_rows.shape[1], o...  235 us
    reduce_scatter x1, waiting for transfers between devices, body(): lax.psum_scatter(arrived[0].astype(jnp.float32).astype(jnp.bfloat16), 're...  84.4 us
    all_to_all x1, waiting for transfers between devices, body(): lax.all_to_all(rounded, 'dev', split_axis=1, concat_axis=0, tiled=True)  58.5 us
    psum x1, waiting for transfers between devices, body(): lax.psum(coeff_terms.astype(jnp.bfloat16), 'rep').astype(jnp.float32)  33.7 us
    all_gather x1, waiting for transfers between devices, body(): returned = lax.all_gather(picked, 'rep', axis=2, tiled=True)  28.9 us
    gather x1, local copies, waits for them, and re-layouts, body(): picked = jnp.take(own_rows, source_unit, axis=0)  13.1 us
  transfers between devices with their start and end apart: 4, of which 4 were waited for; matrix products, arithmetic and copies ran while one was open for 0% of the time, Pallas kernels for 0%

commit v1 on v0

--- a/solution.py
+++ b/solution.py
@@ -62,7 +62,12 @@
     rounded = fresh_start.astype(jnp.bfloat16)
     pieces = lax.all_to_all(rounded, "dev", split_axis=1, concat_axis=0, tiled=True)
     picked = jnp.take(pieces, target, axis=0)
-    returned = lax.all_gather(picked, "rep", axis=2, tiled=True)
+    ring = [picked]
+    for hop in range(3):
+        ring.append(lax.ppermute(ring[-1], "rep", [(dev, (dev + 1) % 4) for dev in range(4)]))
+    returned = jnp.roll(
+        jnp.concatenate(ring[::-1], axis=2), (lax.axis_index("rep") + 1) * ring[0].shape[2], axis=2
+    )
     vec_change = vec_start - vec_summed / rep_count
     vec_new_momentum = outer_momentum * vec_momentum + vec_change
     vec_new = vec_start - outer_rate * (vec_change + outer_momentum * vec_new_momentum)

time: 538 us -> 559 us (1.039)
  blocking collectives: 245 us -> 258 us
    ppermute x0 -> x3, waiting for transfers between devices: none -> 34.2 us  [body(): lax.ppermute(ring[-1], 'rep', [(dev, (dev + 1) % 4) for dev in range(4)])]
    all_gather x1 -> x0, waiting for transfers between devices: 28.9 us -> none  [body(): returned = lax.all_gather(picked, 'rep', axis=2, tiled=True)]
    psum x1, blocking collectives: 10.3 us -> 22.7 us  [body(): lax.psum(vec_terms.astype(jnp.bfloat16), 'rep').astype(jnp.float32)]
  transfers between devices with their start and end apart: 4 -> 6, of which waited for: 4 -> 5; matrix products, arithmetic and copies ran while one was open for 0% -> 0% of each run, Pallas kernels for 0% -> 0%
where the time goes in v1:
time: 559 us
  blocking collectives  258 us (46%)
  waiting for transfers between devices  211 us (38%)
  local copies, waits for them, and re-layouts  40.5 us (7%)
  matrix products  19.7 us (4%)
  between operations  14.2 us (3%)
  other arithmetic  9.61 us (2%)
  starting transfers between devices  5.84 us (1%)
    all_to_all x1, blocking collectives, body(): lax.all_to_all(picked.reshape(dev_count, slot_count, own_rows.shape[1], o...  235 us
    reduce_scatter x1, waiting for transfers between devices, body(): lax.psum_scatter(arrived[0].astype(jnp.float32).astype(jnp.bfloat16), 're...  84.4 us
    all_to_all x1, waiting for transfers between devices, body(): lax.all_to_all(rounded, 'dev', split_axis=1, concat_axis=0, tiled=True)  58.5 us
    ppermute x3, waiting for transfers between devices, body(): lax.ppermute(ring[-1], 'rep', [(dev, (dev + 1) % 4) for dev in range(4)])  34.2 us
    psum x1, waiting for transfers between devices, body(): lax.psum(coeff_terms.astype(jnp.bfloat16), 'rep').astype(jnp.float32)  33.7 us
    psum x1, blocking collectives, body(): lax.psum(vec_terms.astype(jnp.bfloat16), 'rep').astype(jnp.float32)  22.7 us
    gather x1, local copies, waits for them, and re-layouts, body(): picked = jnp.take(own_rows, source_unit, axis=0)  13.1 us
  transfers between devices with their start and end apart: 6, of which 5 were waited for; matrix products, arithmetic and copies ran while one was open for 0% of the time, Pallas kernels for 0%

profile of v1, /device:TPU:0, one launch (start us, length us, event | category | flops | bytes accessed | tf_op | source)
XLA Modules:
  0.0 558.7 jit_solution(5766408001948646869)
XLA Ops:
  7.2 0.9 convert_reduce_fusion
  8.2 0.7 compare_and_fusion.2
  8.9 0.1 select_reduce_fusion
  9.1 0.1 fusion.7
  9.3 13.1 %gather_fusion = bf16[320,16,1024]{2,1,0:T(8,128)(2,1)} fusion(bf16[160,16,1024]{2,1,0:T(8,128)(2,1)} %bitcast.60, s32[1024]{0:T(1024)S(1)} %pad_clamp_fusion.1), kind=kCustom, calls=%fused_computation | custom fusion | bytes 20972800 | tf_op jit(solution)/shard_map/jit(_take)/gather | solution.py:27
  22.4 6.0 %select_select_fusion = bf16[8,40,16,1024]{3,2,1,0:T(8,128)(2,1)S(1)} fusion(bf16[8,40,16,1024]{3,2,1,0:T(8,128)(2,1)} %bitcast.59, pred[8,40]{1,0:T(8,128)(4,1)S(1)} %compare_and_fusion.1, pred[8,40]{1,0:T(8,128)(4,1)S(1)} %broadcast_in_dim.85), kind=kLoop, calls=%fused_computation.2 | loop fusion | flops 10485760 | bytes 20972160 | tf_op jit(solution)/shard_map/jit(_where)/select_n | solution.py:28
  28.3 235.2 %all_to_all.33 = bf16[8,40,16,1024]{3,2,1,0:T(8,128)(2,1)} all-to-all(bf16[8,40,16,1024]{3,2,1,0:T(8,128)(2,1)S(1)} %select_select_fusion), channel_id=1, replica_groups=mesh['rep'=4,'dev'=8] {'dev'}, dimensions={0} | all-to-all | bytes 20971520 | tf_op jit(solution)/shard_map/all_to_all | solution.py:29
  263.5 10.4 %copy.24 = bf16[1,40,8,16,1024]{4,3,2,1,0:T(8,128)(2,1)} copy(bf16[1,40,8,16,1024]{4,3,1,2,0:T(8,128)(2,1)} %bitcast.58) | data formatting | bytes 20971520 | tf_op jit(solution)/shard_map/all_to_all | solution.py:29
  274.0 84.4 %reduce-scatter.2.cloned.1.call-done = bf16[40,128,256]{2,1,0:T(8,128)(2,1)} async-done(((bf16[40,128,1024]{2,1,0:T(8,128)(2,1)}), bf16[40,128,256]{2,1,0:T(8,128)(2,1)}) %reduce-scatter.2.cloned.1.call-update) | async-done | bytes 2621456 | tf_op jit(solution)/shard_map/reduce_scatter | solution.py:36
  358.5 9.5 %fusion.6 = bf16[40,128,64]{1,2,0:T(8,128)(2,1)} fusion(f32[1,40,128,256]{3,2,1,0:T(8,128)} %param.10, bf16[40,128,256]{2,1,0:T(8,128)(2,1)} %reduce-scatter.2.cloned.1.call-done, f32[64,1024]{1,0:T(8,128)S(1)} %copy-done, s32[]{:T(128)S(6)} %select_n.71), kind=kOutput, calls=%fused_computation.14 | convolution fusion | flops 1010892800 | bytes 8585220 | tf_op jit(solution)/shard_map/sbq,kq->sbk/dot_general | solution.py:49
  368.0 0.2 fusion.14
  368.2 33.7 %all-reduce.2.cloned.1.call-done = bf16[40,128,64]{1,2,0:T(8,128)(2,1)} async-done(((bf16[40,128,64]{1,2,0:T(8,128)(2,1)}), bf16[40,128,64]{1,2,0:T(8,128)(2,1)}) %all-reduce.2.cloned.1.call-update) | async-done | bytes 655376 | tf_op jit(solution)/shard_map/psum | solution.py:52
  401.9 10.2 %fusion.1 = (f32[1,40,128,256]{3,2,1,0:T(8,128)}, f32[1,40,128,256]{3,2,1,0:T(8,128)}, bf16[40,128,256]{2,1,0:T(8,128)(2,1)S(1)}) fusion(f32[1,40,128,256]{3,2,1,0:T(8,128)} %param.11, bf16[40,128,256]{2,1,0:T(8,128)(2,1)S(1)} %copy-done.1, f32[1,40,128,256]{3,2,1,0:T(8,128)} %param.10, pred[40]{0:T(512)(128)(4,1)S(1)} %get-tuple-element.5, ...), kind=kOutput, calls=%fused_computation.6 | convolution fusion | flops 1023672320 | bytes 26936324 | tf_op jit(solution)/shard_map/sbk,kq->sbq/dot_general | solution.py:55
  412.1 3.0 copy.25
  415.1 5.7 %all-to-all-start.1 = ((bf16[40,128,256]{2,0,1:T(8,128)(2,1)}), bf16[40,128,256]{2,0,1:T(8,128)(2,1)S(1)}, u32[]{:S(2)}, u32[]{:S(2)}) async-start(bf16[40,128,256]{2,0,1:T(8,128)(2,1)} %copy.25), calls=%async_computation.2 | async-start | bytes 5242880 | tf_op jit(solution)/shard_map/all_to_all | solution.py:63
  420.8 58.5 %all-to-all-done.1 = bf16[40,128,256]{2,0,1:T(8,128)(2,1)S(1)} async-done(((bf16[40,128,256]{2,0,1:T(8,128)(2,1)}), bf16[40,128,256]{2,0,1:T(8,128)(2,1)S(1)}, u32[]{:S(2)}, u32[]{:S(2)}) %all-to-all-start.1) | async-done | bytes 2621472 | tf_op jit(solution)/shard_map/all_to_all | solution.py:63
  479.4 2.1 copy.27
  481.4 2.6 gather_fusion.1
  484.0 0.2 broadcast_select_fusion
  484.3 17.0 %collective-permute-done = bf16[160,16,256]{2,1,0:T(8,128)(2,1)S(1)} collective-permute-done((bf16[160,16,256]{2,1,0:T(8,128)(2,1)S(1)}, bf16[160,16,256]{2,1,0:T(8,128)(2,1)S(1)}, u32[]{:S(2)}, u32[]{:S(2)}) %collective-permute-start) | collective-permute-done | bytes 1310752 | tf_op jit(solution)/shard_map/ppermute | solution.py:67
  501.3 17.1 %collective-permute-done.1 = bf16[160,16,256]{2,1,0:T(8,128)(2,1)} collective-permute-done((bf16[160,16,256]{2,1,0:T(8,128)(2,1)S(1)}, bf16[160,16,256]{2,1,0:T(8,128)(2,1)}, u32[]{:S(2)}, u32[]{:S(2)}) %collective-permute-start.1) | collective-permute-done | bytes 1310752 | tf_op jit(solution)/shard_map/ppermute | solution.py:67
  518.5 22.7 %psum.15 = bf16[13,1024]{1,0:T(8,128)(2,1)S(1)} all-reduce(bf16[13,1024]{1,0:T(8,128)(2,1)S(1)} %bitcast.63), channel_id=1, replica_groups=mesh['rep'=4,'dev'=8] {'rep'}, use_global_device_ids=true, to_apply=%region_7.8 | all-reduce | flops 13312 | bytes 53248 | tf_op jit(solution)/shard_map/psum | solution.py:53
  541.2 0.7 multiply_subtract_fusion
  541.8 1.5 constant_dynamic-update-slice_fusion.7
  543.3 1.5 constant_dynamic-update-slice_fusion.6
  544.8 0.2 constant_dynamic-update-slice_fusion.5
  545.0 0.3 constant_dynamic-update-slice_fusion.4
  545.4 1.5 constant_dynamic-update-slice_fusion.3
  546.9 1.5 constant_dynamic-update-slice_fusion.2
  548.4 0.2 constant_dynamic-update-slice_fusion.1
  548.5 0.3 constant_dynamic-update-slice_fusion
  548.9 2.9 constant_dynamic-slice_fusion
  (26 shorter events, 0.4 us)
Async XLA Ops:
  7.2 351.3 %copy-start = (f32[64,1024]{1,0:T(8,128)S(1)}, f32[64,1024]{1,0:T(8,128)}, u32[]{:S(2)}) copy-start(f32[64,1024]{1,0:T(8,128)} %param.12) | copy-start | bytes 786436
  7.2 351.3 %reduce-scatter.2.cloned.1.call-start = ((), (), s32[]{:S(2)}) async-start(), calls=%async_computation.3 | async-start | bytes 13107200 | tf_op jit(solution)/shard_map/reduce_scatter | solution.py:36
  274.0 127.9 %all-reduce.2.cloned.1.call-start = ((), (), s32[]{:S(2)}) async-start(), calls=%async_computation.4 | async-start | bytes 1310720 | tf_op jit(solution)/shard_map/psum | solution.py:52
  358.5 43.5 %copy-start.1 = (bf16[40,128,256]{2,1,0:T(8,128)(2,1)S(1)}, bf16[40,128,256]{2,1,0:T(8,128)(2,1)}, u32[]{:S(2)}) copy-start(bf16[40,128,256]{2,1,0:T(8,128)(2,1)} %reduce-scatter.2.cloned.1.call-done) | copy-start | bytes 7864324
  415.1 64.3 %all-to-all-start.1 = ((bf16[40,128,256]{2,0,1:T(8,128)(2,1)}), bf16[40,128,256]{2,0,1:T(8,128)(2,1)S(1)}, u32[]{:S(2)}, u32[]{:S(2)}) async-start(bf16[40,128,256]{2,0,1:T(8,128)(2,1)} %copy.25), calls=%async_computation.2 | async-start | bytes 5242880 | tf_op jit(solution)/shard_map/all_to_all | solution.py:63
  479.4 39.1 %copy-start.4 = (bf16[1,13,1024]{2,1,0:T(8,128)(2,1)S(1)}, bf16[1,13,1024]{2,1,0:T(8,128)(2,1)}, u32[]{:S(2)}) copy-start(bf16[1,13,1024]{2,1,0:T(8,128)(2,1)} %param.13) | copy-start | bytes 79876
  479.4 61.8 %copy-start.2 = (f32[13,1024]{1,0:T(8,128)S(1)}, f32[13,1024]{1,0:T(8,128)}, u32[]{:S(2)}) copy-start(f32[13,1024]{1,0:T(8,128)} %param.14) | copy-start | bytes 159748
  479.4 61.8 %copy-start.3 = (f32[13,1024]{1,0:T(8,128)S(1)}, f32[13,1024]{1,0:T(8,128)}, u32[]{:S(2)}) copy-start(f32[13,1024]{1,0:T(8,128)} %param.15) | copy-start | bytes 159748
  484.2 17.1 %collective-permute-start = (bf16[160,16,256]{2,1,0:T(8,128)(2,1)S(1)}, bf16[160,16,256]{2,1,0:T(8,128)(2,1)S(1)}, u32[]{:S(2)}, u32[]{:S(2)}) collective-permute-start(bf16[160,16,256]{2,1,0:T(8,128)(2,1)S(1)} %broadcast_select_fusion), channel_id=1, source_target_pairs={{0,8},{8,16},{16,24},{24,0},{1,9},{9,17},{17,25},{25,1},{2,10},{10... | collective-permute-start | bytes 3932168 | tf_op jit(solution)/shard_map/ppermute | solution.py:67
  501.3 17.1 %collective-permute-start.1 = (bf16[160,16,256]{2,1,0:T(8,128)(2,1)S(1)}, bf16[160,16,256]{2,1,0:T(8,128)(2,1)}, u32[]{:S(2)}, u32[]{:S(2)}) collective-permute-start(bf16[160,16,256]{2,1,0:T(8,128)(2,1)S(1)} %collective-permute-done), channel_id=1, source_target_pairs={{0,8},{8,16},{16,24},{24,0},{1,9},{9,17},{17,25},{25,1},{2,10},{10... | collective-permute-start | bytes 3932168 | tf_op jit(solution)/shard_map/ppermute | solution.py:67
  518.5 23.4 %collective-permute-start.2 = (bf16[160,16,256]{2,1,0:T(8,128)(2,1)}, bf16[160,16,256]{2,1,0:T(8,128)(2,1)}, u32[]{:S(2)}, u32[]{:S(2)}) collective-permute-start(bf16[160,16,256]{2,1,0:T(8,128)(2,1)} %collective-permute-done.1), channel_id=1, source_target_pairs={{0,8},{8,16},{16,24},{24,0},{1,9},{9,17},{17,25},{25,1},{2,10},{10... | collective-permute-start | bytes 3932168 | tf_op jit(solution)/shard_map/ppermute | solution.py:67
Sparse Core Ops, SparseCore 0:
  274.1 84.3 reduce-scatter.1
  368.1 33.7 all-reduce.1
